TPU v7x, 32 devices: a whole 2x2x4 slice. The times are simulated.
32 devices in a mesh: groups: 2 (over x), blk: 16 (over z, y, core).
Axes of the slice: x: 2, y: 2, z: 4, core: 2. Of those that a mesh axis runs over, the one named last changes fastest.
Arguments:
- layer_input_tokens: bfloat16 [384, 8192], P('groups', 'blk'), parts along dimension 0, may hold values from -6 to 6
- input_norm_gain: float32 [8192], replicated, may hold values from 0.5 to 1.5
- query_weight: bfloat16 [8192, 8192], P(None, 'blk'), may hold values from -0.0625 to 0.0625
- key_value_weight: bfloat16 [8192, 2048], P(None, 'blk'), may hold values from -0.0625 to 0.0625
- output_weight: bfloat16 [8192, 8192], P(None, 'blk'), may hold values from -0.5 to 0.5
- adapter_down_weight: bfloat16 [16, 64, 8192], P('blk'), may hold values from -0.0625 to 0.0625
- adapter_up_weight: bfloat16 [16, 64, 8192], P(None, None, 'blk'), may hold values from -0.75 to 0.75
- key_value_page_pool: bfloat16 [512, 128, 2048], P(('groups', 'blk')), parts along dimension 0, may hold values from -240 to 240
- request_adapter: int32 [128], P('groups'), parts along dimension 0, may hold values from 0 to 15
- adapter_storage_slot: int32 [16], replicated, may hold values from 0 to 15, each once
- cached_lengths: int32 [128], P('groups'), parts along dimension 0, may hold values from 1 to 512, as said below
- request_page_tables: int32 [128, 4], P('groups'), parts along dimension 0, may hold values from -1 to 255, as said below
Outputs:
- layer_out: bfloat16 [384, 8192], P('groups', 'blk'), parts along dimension 0
There are 2 independent parts, one for each index of `groups`. A program takes and returns all parts, laid end to end along the dimension named above; an argument that names none is the same for every part. Nothing has to cross between parts.
Inputs may be any that keep to these rules, and one draw needn't show every extreme that they name: `cached_lengths`: each request's cached length; the longest is exactly 512. `request_page_tables`: row r holds ceil(cached_lengths[r] / 128) page numbers first and -1 after them; no page is named twice in the whole table.
All inputs are finite; a program needn't handle non-finite values.
Results may differ from a plain program's by a relative error of at most 0.0085.
The roundings to bfloat16 on the way count: a program that leaves them out, or rounds other values in their place, can miss the bound.
Values may be sent and summed in bfloat16 or wider, within the bound.
No kernel may reach another device: no remote copies, remote signals or barrier semaphores. Data moves between devices by JAX's collectives and lax.ppermute only.
A program may use at most 128 MiB of HBM per device.

v0:
```python
import math
import jax
import jax.numpy as jnp
from jax import lax
from jax.sharding import PartitionSpec as P

QUERY_HEADS = 64
KEY_VALUE_HEADS = 8
HEAD_WIDTH = 128
PAGE_LENGTH = 128
NEW_TOKENS = 3
theta_base = 500000.0
neg_large = -1e30


def apply_rotation(values, token_positions, first_col, rot_limit):
    width_cols = values.shape[1]
    columns = first_col + jnp.arange(width_cols, dtype=jnp.int32)
    pair_index = (columns % HEAD_WIDTH // 2).astype(jnp.float32)
    inverse = jnp.exp(pair_index * (-2.0 * math.log(theta_base) / HEAD_WIDTH))
    angles = token_positions[:, None] * inverse[None, :]
    cos_val = jnp.cos(angles[:, 0::2])
    sine_val = jnp.sin(angles[:, 0::2])
    even_part = values[:, 0::2]
    odd_part = values[:, 1::2]
    turned = jnp.stack(
        [even_part * cos_val - odd_part * sine_val, even_part * sine_val + odd_part * cos_val],
        axis=-1,
    ).reshape(values.shape)
    return jnp.where((columns < rot_limit)[None, :], turned, values)


def normalize(layer_input_tokens, input_norm_gain):
    values = layer_input_tokens.astype(jnp.float32)
    mean_square = jnp.mean(values * values, axis=-1, keepdims=True)
    return (values * lax.rsqrt(mean_square + 1e-05) * input_norm_gain[None, :]).astype(jnp.bfloat16)


def positions_of(cached_lengths):
    steps_row = jnp.arange(NEW_TOKENS, dtype=jnp.int32)
    return (
        jnp.repeat(cached_lengths, NEW_TOKENS) + jnp.tile(steps_row, cached_lengths.shape[0])
    ).astype(jnp.float32)


def to_tokens(request_first_layout):
    request_count = request_first_layout.shape[0]
    trailing_shape = request_first_layout.shape[3:]
    query_group_width = QUERY_HEADS // KEY_VALUE_HEADS
    split_head_shape = request_first_layout.reshape(
        (request_count, KEY_VALUE_HEADS, NEW_TOKENS, query_group_width) + trailing_shape
    )
    order_axes = (0, 2, 1, 3) + tuple(range(4, 4 + len(trailing_shape)))
    return split_head_shape.transpose(order_axes).reshape(request_count * NEW_TOKENS, -1)


def local(
    layer_input_tokens,
    input_norm_gain,
    query_weight,
    key_value_weight,
    output_weight,
    adapter_down_weight,
    adapter_up_weight,
    key_value_page_pool,
    request_adapter,
    adapter_storage_slot,
    cached_lengths,
    request_page_tables,
):
    own_index = lax.axis_index("blk")
    gathered = lax.all_gather(layer_input_tokens, "blk", axis=1, tiled=True)
    normalized_input = normalize(gathered, input_norm_gain)
    request_count = cached_lengths.shape[0]
    adapter_total = adapter_storage_slot.shape[0]
    choose = request_adapter[:, None] == jnp.arange(adapter_total, dtype=jnp.int32)[None, :]
    req_slot = jnp.sum(jnp.where(choose, adapter_storage_slot[None, :], 0), axis=1)
    token_cache_slot = jnp.repeat(req_slot, NEW_TOKENS)
    local_token_count = adapter_down_weight.shape[0]
    local_pick = (
        token_cache_slot[:, None] - own_index * local_token_count
        == jnp.arange(local_token_count, dtype=jnp.int32)[None, :]
    )
    output_projected = jnp.einsum(
        "ly,mxy->lmx", normalized_input, adapter_down_weight, preferred_element_type=jnp.float32
    )
    partial_codes = jnp.sum(jnp.where(local_pick[:, :, None], output_projected, 0.0), axis=1)
    adapter_choice_index = lax.psum(partial_codes, "blk").astype(jnp.bfloat16)
    up_weight_rows = adapter_up_weight[token_cache_slot]
    adapter_query_update = jnp.einsum(
        "gk,gkq->gq", adapter_choice_index, up_weight_rows, preferred_element_type=jnp.float32
    )
    token_positions = positions_of(cached_lengths)
    query_cols = query_weight.shape[1]
    keyval_cols = key_value_weight.shape[1]
    query_part = apply_rotation(
        jnp.dot(normalized_input, query_weight, preferred_element_type=jnp.float32)
        + adapter_query_update,
        token_positions,
        own_index * query_cols,
        QUERY_HEADS * HEAD_WIDTH,
    ).astype(jnp.bfloat16)
    keyval_part = apply_rotation(
        jnp.dot(normalized_input, key_value_weight, preferred_element_type=jnp.float32),
        token_positions,
        own_index * keyval_cols,
        KEY_VALUE_HEADS * HEAD_WIDTH,
    ).astype(jnp.bfloat16)
    query_vectors, key_value_rows = (
        lax.all_gather(query_part, "blk", axis=1, tiled=True),
        lax.all_gather(keyval_part, "blk", axis=1, tiled=True),
    )
    query_group_width = QUERY_HEADS // KEY_VALUE_HEADS
    query_feature_width = query_group_width * NEW_TOKENS
    score_scale = 1.0 / math.sqrt(HEAD_WIDTH)
    query_req = (
        query_vectors.reshape(
            request_count, NEW_TOKENS, KEY_VALUE_HEADS, query_group_width, HEAD_WIDTH
        )
        .transpose(0, 2, 1, 3, 4)
        .reshape(request_count, KEY_VALUE_HEADS, query_feature_width, HEAD_WIDTH)
    )
    fresh_token_rows = key_value_rows.reshape(
        request_count, NEW_TOKENS, 2, KEY_VALUE_HEADS, HEAD_WIDTH
    )
    request_page_count = key_value_page_pool.shape[0]
    table_width = request_page_tables.shape[1]
    page_ids = own_index * request_page_count + jnp.arange(request_page_count, dtype=jnp.int32)
    matches = request_page_tables[None, :, :] == page_ids[:, None, None]
    page_owner = jnp.any(matches, axis=2)
    page_live = jnp.any(page_owner, axis=1)
    page_req = jnp.sum(
        jnp.where(page_owner, jnp.arange(request_count, dtype=jnp.int32)[None, :], 0), axis=1
    )
    page_slot = jnp.sum(
        jnp.where(matches, jnp.arange(table_width, dtype=jnp.int32)[None, None, :], 0), axis=(1, 2)
    )
    page_len = jnp.sum(jnp.where(page_owner, cached_lengths[None, :], 0), axis=1)
    key_pos = page_slot[:, None] * PAGE_LENGTH + jnp.arange(PAGE_LENGTH, dtype=jnp.int32)[None, :]
    key_valid = page_live[:, None] & (key_pos < page_len[:, None])
    valid_full = key_valid[:, None, None, :]
    gathered_cache_pages = key_value_page_pool.reshape(
        request_page_count, PAGE_LENGTH, 2, KEY_VALUE_HEADS, HEAD_WIDTH
    )
    query_page = query_req[page_req]
    scores = (
        jnp.einsum(
            "skqd,spkd->skqp",
            query_page,
            gathered_cache_pages[:, :, 0],
            preferred_element_type=jnp.float32,
        )
        * score_scale
    )
    masked = jnp.where(valid_full, scores, neg_large)
    page_peak = jnp.max(masked, axis=-1)
    req_peak = jnp.max(
        jnp.where(page_owner[:, :, None, None], page_peak[:, None], neg_large), axis=0
    )
    fresh_scores = (
        jnp.einsum(
            "rkqd,rjkd->rkqj",
            query_req,
            fresh_token_rows[:, :, 0],
            preferred_element_type=jnp.float32,
        )
        * score_scale
    )
    step_of = jnp.arange(query_feature_width, dtype=jnp.int32) // query_group_width
    fresh_ok = (jnp.arange(NEW_TOKENS, dtype=jnp.int32)[None, :] <= step_of[:, None])[None, None]
    fresh_masked = jnp.where(fresh_ok, fresh_scores, neg_large)
    top_score = lax.pmax(jnp.maximum(req_peak, jnp.max(fresh_masked, axis=-1)), "blk")
    weights = jnp.where(valid_full, jnp.exp(masked - top_score[page_req][..., None]), 0.0)
    page_num = jnp.einsum(
        "skqp,spkd->skqd",
        weights.astype(jnp.bfloat16),
        gathered_cache_pages[:, :, 1],
        preferred_element_type=jnp.float32,
    )
    owner_frac = page_owner.astype(jnp.float32)
    req_num = jnp.einsum("sr,skqd->rkqd", owner_frac, page_num, precision=lax.Precision.HIGHEST)
    req_den = jnp.einsum(
        "sr,skq->rkq", owner_frac, jnp.sum(weights, axis=-1), precision=lax.Precision.HIGHEST
    )
    fresh_weights = jnp.where(fresh_ok, jnp.exp(fresh_masked - top_score[..., None]), 0.0)
    fresh_num = jnp.einsum(
        "rkqj,rjkd->rkqd",
        fresh_weights.astype(jnp.bfloat16),
        fresh_token_rows[:, :, 1],
        preferred_element_type=jnp.float32,
    )
    fresh_den = jnp.sum(fresh_weights, axis=-1)
    num_tok = to_tokens(req_num)
    den_tok = to_tokens(req_den[..., None])
    fresh_num_tok = to_tokens(fresh_num)
    fresh_den_tok = to_tokens(fresh_den[..., None])
    num_all, den_all = lax.psum((num_tok, den_tok), "blk")
    totals = den_all + fresh_den_tok
    attended = ((num_all + fresh_num_tok) / jnp.repeat(totals, HEAD_WIDTH, axis=1)).astype(
        jnp.bfloat16
    )
    return jnp.dot(attended, output_weight, preferred_element_type=jnp.float32).astype(jnp.bfloat16)


def solution(mesh):
    placed = (
        P("groups", "blk"),
        P(),
        P(None, "blk"),
        P(None, "blk"),
        P(None, "blk"),
        P("blk", None, None),
        P(None, None, "blk"),
        P(("groups", "blk"), None, None),
        P("groups"),
        P(),
        P("groups"),
        P("groups", None),
    )
    return jax.shard_map(
        local, mesh=mesh, in_specs=placed, out_specs=P("groups", "blk"), check_vma=False
    )
```

profile of v0, /device:TPU:0, one launch (start us, length us, event | category | flops | bytes accessed | tf_op | source)
XLA Modules:
  0.0 457.9 jit_solution(6853859499092122322)
XLA Ops:
  6.5 0.7 all-gather.3.cloned.1.call-update
  7.3 0.8 select_reduce_fusion.2
  8.5 0.7 add_convert_fusion
  9.5 7.3 %slice.33 = f32[192,256]{1,0:T(8,128)} slice(f32[192,512]{1,0:T(8,128)S(1)} %broadcast_multiply_fusion), slice={[0:192:1], [0:512:2]} | slice | bytes 393216 | tf_op jit(solution)/shard_map/slice | solution.py:22
  16.8 8.1 %gather_fusion = bf16[192,64,512]{2,1,0:T(8,128)(2,1)} fusion(bf16[16,64,512]{2,1,0:T(8,128)(2,1)S(1)} %copy-done.2, s32[1024]{0:T(1024)S(1)} %pad_clamp_fusion.1), kind=kCustom, calls=%fused_computation | custom fusion | bytes 25166592 | tf_op jit(solution)/shard_map/gather | solution.py:89
  24.9 0.7 fusion.49
  25.6 33.9 %all-gather.3.cloned.1.call-done = bf16[192,8192]{1,0:T(8,128)(2,1)} async-done(((bf16[192,512]{1,0:T(8,128)(2,1)}), bf16[192,8192]{1,0:T(8,128)(2,1)}) %all-gather.3.cloned.1.call-update) | async-done | bytes 3145744 | tf_op jit(solution)/shard_map/all_gather | solution.py:72
  59.5 2.6 fusion
  62.1 3.4 convolution_select_fusion
  65.5 59.2 %psum.21 = bf16[192,64]{0,1:T(8,128)(2,1)S(1)} all-reduce(f32[192,64]{0,1:T(8,128)S(1)} %convolution_select_fusion), channel_id=1, replica_groups=mesh['groups'=2,'blk'=16] {'blk'}, use_global_device_ids=true, to_apply=%region_6.7 | all-reduce | flops 12288 | bytes 73728 | tf_op jit(solution)/shard_map/psum | solution.py:88
  124.8 6.5 %fusion.53 = f32[192,1,512]{2,1,0:T(1,128)S(1)} fusion(bf16[192,64,1]{1,2,0:T(2,128)(2,1)S(1)} %copy.109, bf16[192,64,512]{2,1,0:T(8,128)(2,1)} %gather_fusion), kind=kOutput, calls=%fused_computation.118 | convolution fusion | flops 12582912 | bytes 13000704 | tf_op jit(solution)/shard_map/gk,gkq->gq/dot_general | solution.py:90
  131.3 5.3 %convolution_add_fusion = f32[192,512]{1,0:T(8,128)S(1)} fusion(bf16[8192,512]{1,0:T(8,128)(2,1)} %param.14, f32[192,1,512]{2,1,0:T(1,128)S(1)} %fusion.53, bf16[192,8192]{1,0:T(8,128)(2,1)S(1)} %copy-done.5, f32[8192]{0:T(1024)S(1)} %copy-done.11, f32[192]{0:T(256)S(1)} %add_rsqrt_fusion), kind=kOutput, calls=%fused_computation.28 | convolution fusion | flops 1617002496 | bytes 12354304 | tf_op jit(solution)/shard_map/dot_general | solution.py:97
  136.6 6.7 %slice.32 = f32[192,256]{1,0:T(8,128)S(1)} slice(f32[192,512]{1,0:T(8,128)S(1)} %convolution_add_fusion), slice={[0:192:1], [0:512:2]} | slice | bytes 393216 | tf_op jit(solution)/shard_map/slice | solution.py:24
  143.3 6.6 %slice.34 = f32[192,256]{1,0:T(8,128)S(1)} slice(f32[192,512]{1,0:T(8,128)S(1)} %convolution_add_fusion), slice={[0:192:1], [1:512:2]} | slice | bytes 393216 | tf_op jit(solution)/shard_map/slice | solution.py:25
  150.6 0.7 select_convert_fusion
  151.6 12.3 %copy.94 = bf16[16,128,2048]{1,2,0:T(8,128)(2,1)} copy(bf16[16,128,2048]{2,1,0:T(8,128)(2,1)} %param.19) | data formatting | bytes 16777216 | tf_op args[7]
  164.0 1.7 slice.37
  166.4 0.3 fusion.50
  166.7 3.0 fusion.44
  169.8 1.7 slice.36
  171.4 1.7 slice.38
  173.5 22.5 %all_gather.11 = bf16[192,2048]{1,0:T(8,128)(2,1)S(1)} all-gather(bf16[192,128]{1,0:T(8,128)(2,1)S(1)} %select_convert_fusion.1), channel_id=1, replica_groups=mesh['groups'=2,'blk'=16] {'blk'}, dimensions={1}, use_global_device_ids=true | all-gather | bytes 835584 | tf_op jit(solution)/shard_map/all_gather | solution.py:111
  196.2 0.9 fusion.48
  197.1 2.3 all-gather.5.cloned.1.call-done
  199.4 2.8 copy.117
  202.2 1.8 copy-done.3
  204.0 2.3 copy.139
  206.3 2.6 gather_fusion.1
  208.9 3.5 fusion.51
  212.3 0.5 select_reduce_fusion
  213.0 3.7 fusion.52
  216.7 61.5 %pmax.7 = f32[64,8,24]{2,1,0:T(8,128)S(1)} all-reduce(f32[64,8,24]{2,1,0:T(8,128)S(1)} %max.5), channel_id=1, replica_groups=mesh['groups'=2,'blk'=16] {'blk'}, use_global_device_ids=true, to_apply=%region_11.12 | all-reduce | flops 12288 | bytes 98304 | tf_op jit(solution)/shard_map/pmax | solution.py:172
  278.2 0.6 gather_fusion.2
  278.8 4.5 fusion.9
  283.4 3.1 convolution_bitcast_fusion.1
  286.5 6.3 %copy.102 = f32[64,3,8,8,128]{4,3,2,1,0:T(8,128)} copy(f32[64,3,8,8,128]{4,0,3,1,2:T(8,128)S(1)} %convolution_bitcast_fusion.1) | data formatting | bytes 12582912 | tf_op jit(solution)/shard_map/transpose | solution.py:54
  292.8 7.2 %reshape.302 = f32[192,8192]{1,0:T(8,128)} reshape(f32[64,3,8,8,128]{4,3,2,1,0:T(8,128)} %copy.102) | data formatting | bytes 12582912 | tf_op jit(solution)/shard_map/reshape | solution.py:54
  300.0 1.8 convolution_bitcast_fusion
  301.8 3.3 copy.138
  305.1 7.4 %reshape.304 = f32[192,8192]{1,0:T(8,128)} reshape(f32[64,3,8,8,128]{4,3,2,1,0:T(8,128)} %bitcast.122) | data formatting | bytes 12582912 | tf_op jit(solution)/shard_map/reshape | solution.py:54
  312.6 0.9 fusion.21
  313.7 0.3 copy.108
  314.3 0.9 fusion.11
  316.0 61.4 %psum.23 = f32[192,64]{1,0:T(8,128)S(1)} all-reduce(f32[192,64]{1,0:T(8,128)S(1)} %reshape.306), channel_id=1, replica_groups=mesh['groups'=2,'blk'=16] {'blk'}, use_global_device_ids=true, to_apply=%region_14.15 | all-reduce | flops 12288 | bytes 98304 | tf_op jit(solution)/shard_map/psum | solution.py:197
  377.4 60.1 %all-reduce.2.cloned.1.call-done = f32[192,8192]{1,0:T(8,128)} async-done(((f32[192,8192]{1,0:T(8,128)}), f32[192,8192]{1,0:T(8,128)}) %all-reduce.2.cloned.1.call-update) | async-done | bytes 6291472 | tf_op jit(solution)/shard_map/psum | solution.py:197
  437.5 1.8 broadcast_in_dim.194
  439.3 1.0 copy-done.4
  440.3 10.9 %fusion.13 = bf16[192,512]{1,0:T(8,128)(2,1)} fusion(bf16[8192,512]{1,0:T(8,128)(2,1)} %param.16, f32[24,8,64,128]{3,2,1,0:T(8,128)S(1)} %bitcast.125, f32[192,8192]{1,0:T(8,128)} %all-reduce.2.cloned.1.call-done, f32[192,8192]{1,0:T(8,128)S(1)} %copy-done.4), kind=kOutput, calls=%fused_computation.29 | convolution fusion | flops 1615429632 | bytes 27459584 | tf_op jit(solution)/shard_map/dot_general | solution.py:202
  (74 shorter events, 4.5 us)
Async XLA Ops:
  6.5 160.2 %copy-start = (bf16[8192,128]{1,0:T(8,128)(2,1)S(1)}, bf16[8192,128]{1,0:T(8,128)(2,1)}, u32[]{:S(2)}) copy-start(bf16[8192,128]{1,0:T(8,128)(2,1)} %param.15) | copy-start | bytes 6291460
  6.5 10.3 %copy-start.2 = (bf16[16,64,512]{2,1,0:T(8,128)(2,1)S(1)}, bf16[16,64,512]{2,1,0:T(8,128)(2,1)}, u32[]{:S(2)}) copy-start(bf16[16,64,512]{2,1,0:T(8,128)(2,1)} %param.18) | copy-start | bytes 3145732
  6.5 52.9 %all-gather.3.cloned.1.call-start = ((), (), s32[]{:S(2)}) async-start(), calls=%async_computation | async-start | bytes 3342336 | tf_op jit(solution)/shard_map/all_gather | solution.py:72
  7.3 192.2 %all-gather.5.cloned.1.call-start = ((), (), s32[]{:S(2)}) async-start(), calls=%async_computation.1 | async-start | bytes 3342336 | tf_op jit(solution)/shard_map/all_gather | solution.py:110
  16.8 8.1 %copy-start.6 = (f32[192,256]{1,0:T(8,128)S(1)}, f32[192,256]{1,0:T(8,128)}, u32[]{:S(2)}) copy-start(f32[192,256]{1,0:T(8,128)} %slice.33) | copy-start | bytes 589828
  124.8 6.5 %copy-start.5 = (bf16[192,8192]{1,0:T(8,128)(2,1)S(1)}, bf16[192,8192]{1,0:T(8,128)(2,1)}, u32[]{:S(2)}) copy-start(bf16[192,8192]{1,0:T(8,128)(2,1)} %all-gather.3.cloned.1.call-done) | copy-start | bytes 9437188
  124.8 6.5 %copy-start.11 = (f32[8192]{0:T(1024)S(1)}, f32[8192]{0:T(1024)}, u32[]{:S(2)}) copy-start(f32[8192]{0:T(1024)} %param.13) | copy-start | bytes 98308
  151.3 286.2 %all-reduce.2.cloned.1.call-start = ((), (), s32[]{:S(2)}) async-start(), calls=%async_computation.2 | async-start | bytes 12582912 | tf_op jit(solution)/shard_map/psum | solution.py:197
  151.6 14.2 %copy-start.9 = (s32[64,4]{0,1:T(4,128)S(1)}, s32[64,4]{0,1:T(4,128)}, u32[]{:S(2)}) copy-start(s32[64,4]{0,1:T(4,128)} %param.23) | copy-start | bytes 3076
  151.6 14.3 %copy-start.10 = (s32[64]{0:T(128)S(1)}, s32[64]{0:T(128)}, u32[]{:S(2)}) copy-start(s32[64]{0:T(128)} %param.22) | copy-start | bytes 772
  202.2 1.8 copy-start.3
  278.8 7.7 %copy-start.7 = (f32[16,8,24]{2,1,0:T(8,128)}, f32[16,8,24]{2,1,0:T(8,128)S(1)}, u32[]{:S(2)}) copy-start(f32[16,8,24]{2,1,0:T(8,128)S(1)} %gather_fusion.2) | copy-start | bytes 36868
  305.1 9.1 %copy-start.8 = (f32[16,8,24]{2,1,0:T(8,128)S(1)}, f32[16,8,24]{2,1,0:T(8,128)}, u32[]{:S(2)}) copy-start(f32[16,8,24]{2,1,0:T(8,128)} %copy-done.7) | copy-start | bytes 36868
  437.5 2.8 copy-start.4
  440.3 10.9 %copy-start.1 = (bf16[8192,128]{1,0:T(8,128)(2,1)S(1)}, bf16[8192,128]{1,0:T(8,128)(2,1)}, u32[]{:S(2)}) copy-start(bf16[8192,128]{1,0:T(8,128)(2,1)} %param.15) | copy-start | bytes 6291460
Sparse Core Ops, SparseCore 0:
  9.5 49.8 all-gather.2
  151.4 47.9 all-gather.4
  300.1 137.3 all-reduce.1
where the time goes:
time: 464 us; the launch traced here: 458 us
  blocking collectives  205 us (44%)
  waiting for transfers between devices  97 us (21%)
  local copies, waits for them, and re-layouts  88.1 us (19%)
  matrix products  45.9 us (10%)
  between operations  13.7 us (3%)
  other arithmetic  8.25 us (2%)
    pmax x1, blocking collectives, local(): lax.pmax(jnp.maximum(req_peak, jnp.max(fresh_masked, axis=-1)), 'blk')  61.5 us
    psum x1, blocking collectives, local(): num_all, den_all = lax.psum((num_tok, den_tok), 'blk')  61.4 us
    psum x1, waiting for transfers between devices, local(): num_all, den_all = lax.psum((num_tok, den_tok), 'blk')  60.1 us
    psum x1, blocking collectives, local(): adapter_choice_index = lax.psum(partial_codes, 'blk').astype(jnp.bfloat16)  59.2 us
    all_gather x1, waiting for transfers between devices, local(): gathered = lax.all_gather(layer_input_tokens, 'blk', axis=1, tiled=True)  33.9 us
    all_gather x1, blocking collectives, local(): lax.all_gather(keyval_part, 'blk', axis=1, tiled=True)  22.5 us
    unnamed x27, local copies, waits for them, and re-layouts  18 us
    reshape x4, local copies, waits for them, and re-layouts, to_tokens(): split_head_shape.transpose(order_axes)  15.1 us
  transfers between devices with their start and end apart: 3, of which 3 were waited for; matrix products, arithmetic and copies ran while one was open for 12% of the time, Pallas kernels for 0%

commit v1 on v0

--- a/solution.py
+++ b/solution.py
@@ -1,8 +1,10 @@
+import functools
 import math
 import jax
 import jax.numpy as jnp
 from jax import lax
 from jax.sharding import PartitionSpec as P
+from jax.lax import all_gather
 
 QUERY_HEADS = 64
 KEY_VALUE_HEADS = 8
@@ -11,6 +13,14 @@
 NEW_TOKENS = 3
 theta_base = 500000.0
 neg_large = -1e30
+
+
+def zone_follow(chunk, dev_axis):
+    w_next = jnp.sum(all_gather(chunk, dev_axis), 0)
+    return w_next
+
+
+_prepare_sizes = functools.partial(zone_follow, dev_axis="blk")
 
 
 def apply_rotation(values, token_positions, first_col, rot_limit):
@@ -85,7 +95,7 @@
         "ly,mxy->lmx", normalized_input, adapter_down_weight, preferred_element_type=jnp.float32
     )
     partial_codes = jnp.sum(jnp.where(local_pick[:, :, None], output_projected, 0.0), axis=1)
-    adapter_choice_index = lax.psum(partial_codes, "blk").astype(jnp.bfloat16)
+    adapter_choice_index = _prepare_sizes(partial_codes).astype(jnp.bfloat16)
     up_weight_rows = adapter_up_weight[token_cache_slot]
     adapter_query_update = jnp.einsum(
         "gk,gkq->gq", adapter_choice_index, up_weight_rows, preferred_element_type=jnp.float32

time: 464 us -> 430 us (0.927)
  blocking collectives: 205 us -> 169 us
    psum x1 -> x0, blocking collectives: 59.2 us -> none  [local(): adapter_choice_index = lax.psum(partial_codes, 'blk').astype(jnp.bfloat16)]
    all_gather x0 -> x1, blocking collectives: none -> 21.8 us  [zone_follow(): w_next = jnp.sum(all_gather(chunk, dev_axis), 0)]
    unnamed x27 -> x29, local copies, waits for them, and re-layouts: 18 us -> 18 us
  transfers between devices with their start and end apart: 3 -> 3, of which waited for: 3 -> 3; matrix products, arithmetic and copies ran while one was open for 12% -> 14% of each run, Pallas kernels for 0% -> 0%
where the time goes in v1:
time: 430 us; the launch traced here: 423 us
  blocking collectives  169 us (39%)
  waiting for transfers between devices  96.8 us (23%)
  local copies, waits for them, and re-layouts  88.8 us (21%)
  matrix products  46 us (11%)
  between operations  13.8 us (3%)
  other arithmetic  8.31 us (2%)
    pmax x1, blocking collectives, local(): lax.pmax(jnp.maximum(req_peak, jnp.max(fresh_masked, axis=-1)), 'blk')  62.8 us
    psum x1, blocking collectives, local(): num_all, den_all = lax.psum((num_tok, den_tok), 'blk')  61.3 us
    psum x1, waiting for transfers between devices, local(): num_all, den_all = lax.psum((num_tok, den_tok), 'blk')  60.1 us
    all_gather x1, waiting for transfers between devices, local(): gathered = lax.all_gather(layer_input_tokens, 'blk', axis=1, tiled=True)  33.2 us
    all_gather x1, blocking collectives, local(): lax.all_gather(keyval_part, 'blk', axis=1, tiled=True)  23.6 us
    all_gather x1, blocking collectives, zone_follow(): w_next = jnp.sum(all_gather(chunk, dev_axis), 0)  21.8 us
    unnamed x29, local copies, waits for them, and re-layouts  18 us
    reshape x4, local copies, waits for them, and re-layouts, to_tokens(): split_head_shape.transpose(order_axes)  15.1 us
  transfers between devices with their start and end apart: 3, of which 3 were waited for; matrix products, arithmetic and copies ran while one was open for 14% of the time, Pallas kernels for 0%

profile of v1, /device:TPU:0, one launch (start us, length us, event | category | flops | bytes accessed | tf_op | source)
XLA Modules:
  0.0 423.3 jit_solution(4636294581598989073)
XLA Ops:
  6.5 0.7 all-gather.5.cloned.1.call-update
  7.3 0.8 select_reduce_fusion.2
  8.5 0.7 add_convert_fusion
  9.5 7.3 %slice.33 = f32[192,256]{1,0:T(8,128)} slice(f32[192,512]{1,0:T(8,128)S(1)} %broadcast_multiply_fusion), slice={[0:192:1], [0:512:2]} | slice | bytes 393216 | tf_op jit(solution)/shard_map/slice | solution.py:32
  16.8 8.1 %gather_fusion = bf16[192,64,512]{2,1,0:T(8,128)(2,1)} fusion(bf16[16,64,512]{2,1,0:T(8,128)(2,1)S(1)} %copy-done.2, s32[1024]{0:T(1024)S(1)} %pad_clamp_fusion.1), kind=kCustom, calls=%fused_computation | custom fusion | bytes 25166592 | tf_op jit(solution)/shard_map/gather | solution.py:99
  24.9 1.4 fusion.50
  26.3 33.2 %all-gather.5.cloned.1.call-done = bf16[192,8192]{1,0:T(8,128)(2,1)} async-done(((bf16[192,512]{1,0:T(8,128)(2,1)}), bf16[192,8192]{1,0:T(8,128)(2,1)}) %all-gather.5.cloned.1.call-update) | async-done | bytes 3145744 | tf_op jit(solution)/shard_map/all_gather | solution.py:82
  59.5 2.6 fusion
  62.1 3.4 fusion.16
  65.5 21.8 %all-gather.1 = f32[16,192,64]{1,2,0:T(8,128)S(1)} all-gather(f32[1,192,64]{1,2,0:T(8,128)S(1)} %fusion.16), channel_id=2, replica_groups=mesh['groups'=2,'blk'=16] {'blk'}, dimensions={0}, use_global_device_ids=true | all-gather | bytes 835584 | tf_op jit(solution)/shard_map/all_gather | solution.py:19
  87.5 6.5 %fusion.54 = f32[192,1,512]{2,1,0:T(1,128)S(1)} fusion(bf16[192,64,1]{1,2,0:T(2,128)(2,1)S(1)} %copy.109, bf16[192,64,512]{2,1,0:T(8,128)(2,1)} %gather_fusion), kind=kOutput, calls=%fused_computation.119 | convolution fusion | flops 12582912 | bytes 13000704 | tf_op jit(solution)/shard_map/gk,gkq->gq/dot_general | solution.py:100
  93.9 5.4 %convolution_add_fusion = f32[192,512]{1,0:T(8,128)S(1)} fusion(bf16[8192,512]{1,0:T(8,128)(2,1)} %param.14, f32[192,1,512]{2,1,0:T(1,128)S(1)} %fusion.54, bf16[192,8192]{1,0:T(8,128)(2,1)S(1)} %copy-done.5, f32[8192]{0:T(1024)S(1)} %copy-done.12, f32[192]{0:T(256)S(1)} %add_rsqrt_fusion), kind=kOutput, calls=%fused_computation.28 | convolution fusion | flops 1617002496 | bytes 12354304 | tf_op jit(solution)/shard_map/dot_general | solution.py:107
  99.3 6.7 %slice.32 = f32[192,256]{1,0:T(8,128)S(1)} slice(f32[192,512]{1,0:T(8,128)S(1)} %convolution_add_fusion), slice={[0:192:1], [0:512:2]} | slice | bytes 393216 | tf_op jit(solution)/shard_map/slice | solution.py:34
  106.0 6.6 %slice.34 = f32[192,256]{1,0:T(8,128)S(1)} slice(f32[192,512]{1,0:T(8,128)S(1)} %convolution_add_fusion), slice={[0:192:1], [1:512:2]} | slice | bytes 393216 | tf_op jit(solution)/shard_map/slice | solution.py:35
  113.3 0.7 select_convert_fusion
  114.3 12.3 %copy.94 = bf16[16,128,2048]{1,2,0:T(8,128)(2,1)} copy(bf16[16,128,2048]{2,1,0:T(8,128)(2,1)} %param.19) | data formatting | bytes 16777216 | tf_op args[7]
  126.7 1.7 slice.37
  129.1 0.3 fusion.51
  129.4 3.0 fusion.45
  132.4 1.7 slice.36
  134.1 1.7 slice.38
  136.2 23.6 %all_gather.19 = bf16[192,2048]{1,0:T(8,128)(2,1)S(1)} all-gather(bf16[192,128]{1,0:T(8,128)(2,1)S(1)} %select_convert_fusion.1), channel_id=1, replica_groups=mesh['groups'=2,'blk'=16] {'blk'}, dimensions={1}, use_global_device_ids=true | all-gather | bytes 835584 | tf_op jit(solution)/shard_map/all_gather | solution.py:121
  160.0 0.9 fusion.49
  160.9 2.7 all-gather.7.cloned.1.call-done
  163.6 2.8 copy.117
  166.4 1.8 copy-done.3
  168.2 2.3 copy.139
  170.5 2.6 gather_fusion.1
  173.1 3.5 fusion.52
  176.5 0.5 select_reduce_fusion
  177.2 3.7 fusion.53
  180.9 62.8 %pmax.7 = f32[64,8,24]{2,1,0:T(8,128)S(1)} all-reduce(f32[64,8,24]{2,1,0:T(8,128)S(1)} %max.5), channel_id=1, replica_groups=mesh['groups'=2,'blk'=16] {'blk'}, use_global_device_ids=true, to_apply=%region_11.12 | all-reduce | flops 12288 | bytes 98304 | tf_op jit(solution)/shard_map/pmax | solution.py:182
  243.7 0.6 gather_fusion.2
  244.3 4.5 %fusion.9 = f32[8,3,8,128,16]{3,2,1,0,4:T(8,128)S(1)} fusion(bf16[16,128,2,8,128]{1,4,3,2,0:T(8,128)(2,1)} %bitcast.123, f32[16,8,24,128]{3,2,1,0:T(8,128)S(1)} %get-tuple-element.20, f32[16,8,24]{2,1,0:T(8,128)S(1)} %gather_fusion.2, pred[16,128]{1,0:T(8,128)(4,1)S(1)} %fusion.30), kind=kOutput, calls=%fused_computation.23 | convolution fusion | flops 101842944 | bytes 7354368 | tf_op jit(solution)/shard_map/skqp,spkd->skqd/dot_general | solution.py:184
  248.8 3.1 convolution_bitcast_fusion.1
  251.9 6.3 %copy.102 = f32[64,3,8,8,128]{4,3,2,1,0:T(8,128)} copy(f32[64,3,8,8,128]{4,0,3,1,2:T(8,128)S(1)} %convolution_bitcast_fusion.1) | data formatting | bytes 12582912 | tf_op jit(solution)/shard_map/transpose | solution.py:64
  258.2 7.2 %reshape.303 = f32[192,8192]{1,0:T(8,128)} reshape(f32[64,3,8,8,128]{4,3,2,1,0:T(8,128)} %copy.102) | data formatting | bytes 12582912 | tf_op jit(solution)/shard_map/reshape | solution.py:64
  265.4 1.8 convolution_bitcast_fusion
  267.3 3.3 copy.138
  270.6 7.4 %reshape.305 = f32[192,8192]{1,0:T(8,128)} reshape(f32[64,3,8,8,128]{4,3,2,1,0:T(8,128)} %bitcast.124) | data formatting | bytes 12582912 | tf_op jit(solution)/shard_map/reshape | solution.py:64
  278.0 0.9 fusion.22
  279.1 0.3 copy.108
  279.7 0.9 fusion.11
  281.5 61.3 %psum.15 = f32[192,64]{1,0:T(8,128)S(1)} all-reduce(f32[192,64]{1,0:T(8,128)S(1)} %reshape.307), channel_id=1, replica_groups=mesh['groups'=2,'blk'=16] {'blk'}, use_global_device_ids=true, to_apply=%region_14.15 | all-reduce | flops 12288 | bytes 98304 | tf_op jit(solution)/shard_map/psum | solution.py:207
  342.8 60.1 %all-reduce.2.cloned.1.call-done = f32[192,8192]{1,0:T(8,128)} async-done(((f32[192,8192]{1,0:T(8,128)}), f32[192,8192]{1,0:T(8,128)}) %all-reduce.2.cloned.1.call-update) | async-done | bytes 6291472 | tf_op jit(solution)/shard_map/psum | solution.py:207
  402.9 1.8 broadcast_in_dim.194
  404.7 1.0 copy-done.4
  405.7 10.9 %fusion.13 = bf16[192,512]{1,0:T(8,128)(2,1)} fusion(bf16[8192,512]{1,0:T(8,128)(2,1)} %param.16, f32[24,8,64,128]{3,2,1,0:T(8,128)S(1)} %bitcast.127, f32[192,8192]{1,0:T(8,128)} %all-reduce.2.cloned.1.call-done, f32[192,8192]{1,0:T(8,128)S(1)} %copy-done.4), kind=kOutput, calls=%fused_computation.29 | convolution fusion | flops 1615429632 | bytes 27459584 | tf_op jit(solution)/shard_map/dot_general | solution.py:212
  (77 shorter events, 4.6 us)
Async XLA Ops:
  6.5 122.9 %copy-start = (bf16[8192,128]{1,0:T(8,128)(2,1)S(1)}, bf16[8192,128]{1,0:T(8,128)(2,1)}, u32[]{:S(2)}) copy-start(bf16[8192,128]{1,0:T(8,128)(2,1)} %param.15) | copy-start | bytes 6291460
  6.5 10.3 %copy-start.2 = (bf16[16,64,512]{2,1,0:T(8,128)(2,1)S(1)}, bf16[16,64,512]{2,1,0:T(8,128)(2,1)}, u32[]{:S(2)}) copy-start(bf16[16,64,512]{2,1,0:T(8,128)(2,1)} %param.18) | copy-start | bytes 3145732
  6.5 52.9 %all-gather.5.cloned.1.call-start = ((), (), s32[]{:S(2)}) async-start(), calls=%async_computation | async-start | bytes 3342336 | tf_op jit(solution)/shard_map/all_gather | solution.py:82
  7.3 156.4 %all-gather.7.cloned.1.call-start = ((), (), s32[]{:S(2)}) async-start(), calls=%async_computation.1 | async-start | bytes 3342336 | tf_op jit(solution)/shard_map/all_gather | solution.py:120
  16.8 8.1 %copy-start.6 = (f32[192,256]{1,0:T(8,128)S(1)}, f32[192,256]{1,0:T(8,128)}, u32[]{:S(2)}) copy-start(f32[192,256]{1,0:T(8,128)} %slice.33) | copy-start | bytes 589828
  87.4 6.5 %copy-start.5 = (bf16[192,8192]{1,0:T(8,128)(2,1)S(1)}, bf16[192,8192]{1,0:T(8,128)(2,1)}, u32[]{:S(2)}) copy-start(bf16[192,8192]{1,0:T(8,128)(2,1)} %all-gather.5.cloned.1.call-done) | copy-start | bytes 9437188
  87.4 6.5 %copy-start.12 = (f32[8192]{0:T(1024)S(1)}, f32[8192]{0:T(1024)}, u32[]{:S(2)}) copy-start(f32[8192]{0:T(1024)} %param.13) | copy-start | bytes 98308
  93.9 18.7 %copy-start.7 = (f32[192,256]{1,0:T(8,128)S(1)}, f32[192,256]{1,0:T(8,128)}, u32[]{:S(2)}) copy-start(f32[192,256]{1,0:T(8,128)} %get-tuple-element.16) | copy-start | bytes 589828
  114.0 288.9 %all-reduce.2.cloned.1.call-start = ((), (), s32[]{:S(2)}) async-start(), calls=%async_computation.2 | async-start | bytes 12582912 | tf_op jit(solution)/shard_map/psum | solution.py:207
  114.3 14.2 %copy-start.10 = (s32[64,4]{0,1:T(4,128)S(1)}, s32[64,4]{0,1:T(4,128)}, u32[]{:S(2)}) copy-start(s32[64,4]{0,1:T(4,128)} %param.23) | copy-start | bytes 3076
  114.3 14.3 %copy-start.11 = (s32[64]{0:T(128)S(1)}, s32[64]{0:T(128)}, u32[]{:S(2)}) copy-start(s32[64]{0:T(128)} %param.22) | copy-start | bytes 772
  166.4 1.8 copy-start.3
  244.3 7.7 %copy-start.8 = (f32[16,8,24]{2,1,0:T(8,128)}, f32[16,8,24]{2,1,0:T(8,128)S(1)}, u32[]{:S(2)}) copy-start(f32[16,8,24]{2,1,0:T(8,128)S(1)} %gather_fusion.2) | copy-start | bytes 36868
  270.6 9.1 %copy-start.9 = (f32[16,8,24]{2,1,0:T(8,128)S(1)}, f32[16,8,24]{2,1,0:T(8,128)}, u32[]{:S(2)}) copy-start(f32[16,8,24]{2,1,0:T(8,128)} %copy-done.8) | copy-start | bytes 36868
  402.9 2.8 copy-start.4
  405.7 10.9 %copy-start.1 = (bf16[8192,128]{1,0:T(8,128)(2,1)S(1)}, bf16[8192,128]{1,0:T(8,128)(2,1)}, u32[]{:S(2)}) copy-start(bf16[8192,128]{1,0:T(8,128)(2,1)} %param.15) | copy-start | bytes 6291460
Sparse Core Ops, SparseCore 0:
  9.5 49.8 all-gather.4
  114.2 49.4 all-gather.6
  265.5 137.3 all-reduce.1
